TPU v7x, 256 devices: a whole 4x4x8 slice. The times are simulated.
256 devices in a mesh: section: 2 (over core), seq: 32 (over z, x), cfg: 4 (over y).
Axes of the slice: x: 4, y: 4, z: 8, core: 2. Of those that a mesh axis runs over, the one named last changes fastest.
Arguments:
- hidden_states: bfloat16 [4, 4, 512, 3072], P('cfg', None, 'seq'), may hold values from -250 to 250
- latent: float32 [2, 4, 512, 64], P('section', None, 'seq'), may hold values from -6 to 6
- stale_cache: bfloat16 [2, 4, 32, 2048, 128], P('section', 'cfg', 'seq'), may hold values from -140 to 140
- qkv_weight: bfloat16 [2, 3072, 3, 2048], P('section', None, None, 'cfg'), may hold values from -0.109375 to 0.109375
- out_weight: bfloat16 [2, 3072, 2048], P('section', 'seq', 'cfg'), may hold values from -0.125 to 0.125
- modulation: float32 [2, 6, 3072], P('section'), may hold values from -2.5 to 2.5
- out_modulation: float32 [2, 3072], replicated, may hold values from -2.5 to 2.5
- proj_weight: bfloat16 [3072, 64], replicated, may hold values from -0.109375 to 0.109375
- solver_coef: float32 [2, 3], P('section'), may hold values from 0.5 to 2
- video_len: int32 [2], replicated, may hold values from 911 to 1822, as said below
- text_len: int32 [4], replicated, may hold values from 1 to 226, as said below
- positions: int32 [3, 2, 4, 512], P(None, None, None, 'seq'), may hold values from 0 to 47
Outputs:
- new_latent: float32 [2, 4, 512, 64], P('section', None, 'seq')
- new_cache: bfloat16 [2, 4, 32, 2048, 128], P('section', 'cfg', 'seq')
Inputs may be any that keep to these rules, and one draw needn't show every extreme that they name: `video_len`: in every draw one request has exactly 1822 video tokens. `text_len`: in every draw some sequence has all 226 text tokens live.
All inputs are finite; a program needn't handle non-finite values.
Results may differ from a plain program's by a relative error of at most 0.02.
Values may be sent and summed in bfloat16 or wider, within the bound.
No kernel may reach another device: no remote copies, remote signals or barrier semaphores. Data moves between devices by JAX's collectives and lax.ppermute only.
A program may use at most 128 MiB of HBM per device.

v0:
```python
import math
import jax
import jax.numpy as jnp
from jax import lax
from jax.sharding import PartitionSpec as P

HD = 64
TEXT = 226


def from_behind(value, axis, steps):
    count = lax.axis_size(axis)
    pairs = [(source, (source + steps) % count) for source in range(count)]
    return lax.ppermute(value, axis, pairs)


def row_norm(values):
    centered = values - jnp.mean(values, axis=-1, keepdims=True)
    return centered * lax.rsqrt(jnp.mean(centered * centered, axis=-1, keepdims=True) + 1e-05)


def head_norm(values):
    centered = values - jnp.mean(values, axis=-1, keepdims=True)
    return centered * lax.rsqrt(jnp.mean(centered * centered, axis=-1, keepdims=True) + 1e-06)


def rope_angles(places, head_size):
    half_size = head_size // 2
    pairs_t = head_size // 8
    pairs_h = (half_size - pairs_t) // 2
    pair_index = jnp.arange(half_size)
    first_part = pair_index < pairs_t
    second_part = jnp.logical_and(pair_index >= pairs_t, pair_index < pairs_t + pairs_h)
    third_part = pair_index >= pairs_t + pairs_h
    local_index = jnp.where(
        first_part,
        pair_index,
        jnp.where(second_part, pair_index - pairs_t, pair_index - pairs_t - pairs_h),
    )
    axis_span = jnp.where(first_part, 2 * pairs_t, 2 * pairs_h)
    frequency = jnp.exp(
        -math.log(10000.0) * 2.0 * local_index.astype(jnp.float32) / axis_span.astype(jnp.float32)
    )
    angles = places[0][..., None] * first_part.astype(jnp.float32)
    angles = angles + places[1][..., None] * second_part.astype(jnp.float32)
    angles = angles + places[2][..., None] * third_part.astype(jnp.float32)
    return angles * frequency


def rotate(values, cos_table, sin_table):
    half_size = values.shape[-1] // 2
    first_half = values[..., :half_size]
    second_half = values[..., half_size:]
    return jnp.concatenate(
        [
            first_half * cos_table - second_half * sin_table,
            second_half * cos_table + first_half * sin_table,
        ],
        axis=-1,
    )


def per_device(
    hidden_states,
    latent,
    stale_cache,
    qkv_weight,
    out_weight,
    modulation,
    out_modulation,
    proj_weight,
    solver_coef,
    video_len,
    text_len,
    positions,
):
    section_id = lax.axis_index("section")
    shard_id = lax.axis_index("seq")
    seq_devices = lax.axis_size("seq")
    cfg_devices = lax.axis_size("cfg")
    patches = hidden_states.shape[1]
    patch_dev = hidden_states.shape[2]
    width = hidden_states.shape[3]
    patch_len = patch_dev * seq_devices
    total_len = patch_len * patches
    group_heads = qkv_weight.shape[3] // HD
    seq_count = cfg_devices
    qkv_full = qkv_weight[0].reshape(width, 3, group_heads, HD)
    out_full = lax.all_gather(out_weight[0], "seq", axis=0, tiled=True).reshape(
        width, group_heads, HD
    )
    mod_rows = modulation[0]
    stale_rows = stale_cache[0, 0, 0]
    my_sequence = shard_id // group_heads
    row_ids = jnp.arange(total_len)
    text_limit = lax.dynamic_index_in_dim(text_len, my_sequence, keepdims=False)
    video_limit = lax.dynamic_index_in_dim(video_len, my_sequence // 2, keepdims=False)
    live_keys = jnp.where(row_ids < TEXT, row_ids < text_limit, row_ids - TEXT < video_limit)
    key_patch = row_ids // patch_len
    use_fresh = key_patch[None, :] <= jnp.arange(patches)[:, None]
    scale_factor = HD ** (-0.5)
    row_place = (
        jnp.arange(patches)[:, None] * patch_len
        + shard_id * patch_dev
        + jnp.arange(patch_dev)[None, :]
    )
    text_rows = (row_place < TEXT)[:, :, None]
    shift_rows = jnp.where(text_rows, mod_rows[3], mod_rows[0])
    scale_rows = jnp.where(text_rows, mod_rows[4], mod_rows[1])
    gate_rows = jnp.where(text_rows, mod_rows[5], mod_rows[2])
    angles = rope_angles(positions.astype(jnp.float32), HD)
    angles = jnp.where(text_rows[None], 0.0, angles)
    angles = jnp.repeat(angles, 2, axis=0)[:, None]
    cos_table = jnp.cos(angles)
    sin_table = jnp.sin(angles)

    def run(hidden):
        normed = row_norm(hidden.astype(jnp.float32))
        mixed_rows = (normed * (1.0 + scale_rows) + shift_rows).astype(jnp.bfloat16)
        mixed_rows = lax.all_gather(mixed_rows, "cfg", axis=0, tiled=True)
        projected = jnp.einsum(
            "spqd,djge->sgjpqe", mixed_rows, qkv_full, preferred_element_type=jnp.float32
        )
        queries = rotate(head_norm(projected[:, :, 0]), cos_table, sin_table)
        key_part = rotate(head_norm(projected[:, :, 1]), cos_table, sin_table)
        stacked = jnp.stack([queries, key_part, projected[:, :, 2]], axis=2).astype(jnp.bfloat16)
        outgoing = stacked.reshape(seq_count * group_heads, 3, patches, patch_dev * HD)
        incoming = lax.all_to_all(outgoing, "seq", split_axis=0, concat_axis=3, tiled=True)
        incoming = incoming.reshape(3, patches, patch_len, HD)
        fresh_rows = jnp.concatenate([incoming[1], incoming[2]], axis=-1).reshape(total_len, 2 * HD)
        key_rows = jnp.where(use_fresh[:, :, None], fresh_rows[None], stale_rows[None])
        scores = (
            jnp.einsum(
                "pqe,pke->pqk", incoming[0], key_rows[..., :HD], preferred_element_type=jnp.float32
            )
            * scale_factor
        )
        scores = jnp.where(live_keys[None, None, :], scores, -jnp.inf)
        row_max = jnp.max(scores, axis=-1, keepdims=True)
        weights = jnp.exp(scores - row_max)
        row_sum = jnp.sum(weights, axis=-1, keepdims=True)
        combined = jnp.einsum(
            "pqk,pke->pqe",
            weights.astype(jnp.bfloat16),
            key_rows[..., HD:],
            preferred_element_type=jnp.float32,
        )
        attended = (combined / row_sum).astype(jnp.bfloat16)
        attended = attended.reshape(patches, seq_devices, patch_dev * HD)[None]
        returned = lax.all_to_all(attended, "seq", split_axis=2, concat_axis=0, tiled=True)
        returned = returned.reshape(seq_count, group_heads, patches, patch_dev, HD)
        update = lax.psum_scatter(
            jnp.einsum("sgpqe,dge->spqd", returned, out_full, preferred_element_type=jnp.float32),
            "cfg",
            scatter_dimension=0,
            tiled=True,
        )
        result = (hidden.astype(jnp.float32) + gate_rows * update).astype(jnp.bfloat16)
        return (result, fresh_rows)

    first_out, first_cache = run(hidden_states)
    received = from_behind(first_out, "section", 1)
    second_out, second_cache = run(received)
    key_cache = jnp.where(section_id == 0, first_cache, second_cache)
    normed = row_norm(second_out.astype(jnp.float32))
    normed_out = (normed * (1.0 + out_modulation[1]) + out_modulation[0]).astype(jnp.bfloat16)
    predicted = jnp.einsum(
        "spqd,do->spqo", normed_out, proj_weight, preferred_element_type=jnp.float32
    )
    predicted_all = lax.all_gather(predicted, ("section", "cfg"), axis=0, tiled=True)
    predicted_all = predicted_all[predicted_all.shape[0] - seq_count :]
    pair_rows = lax.dynamic_slice_in_dim(predicted_all, 2 * section_id, 2, 0)
    solver_row = solver_coef[0]
    guided = pair_rows[0] + solver_row[2] * (pair_rows[1] - pair_rows[0])
    new_latent = solver_row[0] * latent[0] + solver_row[1] * guided
    return (new_latent[None], key_cache[None, None, None])


def solution(mesh):
    return jax.shard_map(
        per_device,
        mesh=mesh,
        in_specs=(
            P("cfg", None, "seq", None),
            P("section", None, "seq", None),
            P("section", "cfg", "seq", None, None),
            P("section", None, None, "cfg"),
            P("section", "seq", "cfg"),
            P("section", None, None),
            P(),
            P(),
            P("section", None),
            P(),
            P(),
            P(None, None, None, "seq"),
        ),
        out_specs=(P("section", None, "seq", None), P("section", "cfg", "seq", None, None)),
        check_vma=False,
    )
```

profile of v0, /device:TPU:1, one launch (start us, length us, event | category | flops | bytes accessed | tf_op | source)
XLA Modules:
  0.0 396.4 jit_solution(5097558336061669999)
XLA Ops:
  14.1 12.7 %copy.39 = bf16[1,3072,3,512]{1,3,2,0:T(8,128)(2,1)} copy(bf16[1,3072,3,512]{3,1,2,0:T(8,128)(2,1)} %param.15) | data formatting | bytes 18874368 | tf_op args[3]
  27.2 19.9 %all-gather.6.cloned.1.call-done = bf16[4,4,16,3072]{3,2,1,0:T(8,128)(2,1)} async-done(((bf16[1,4,16,3072]{3,2,1,0:T(8,128)(2,1)}), bf16[4,4,16,3072]{3,2,1,0:T(8,128)(2,1)}) %all-gather.6.cloned.1.call-update) | async-done | bytes 1572880 | tf_op jit(solution)/shard_map/all_gather | solution.py:120
  47.1 8.1 %convolution_bitcast_fusion.3 = f32[4,8,3,4,16,64]{5,4,1,2,3,0:T(8,128)S(1)} fusion(bf16[3072,3,8,64,1,1]{0,3,2,1,5,4:T(8,128)(2,1)} %bitcast.167, bf16[4,4,16,3072]{3,2,1,0:T(8,128)(2,1)} %all-gather.6.cloned.1.call-done), kind=kOutput, calls=%fused_computation.19 | convolution fusion | flops 2415919104 | bytes 12582912 | tf_op jit(solution)/shard_map/spqd,djge->sgjpqe/dot_general | solution.py:121
  62.9 9.5 %all-to-all-start = ((bf16[32,3,4,1024]{3,2,1,0:T(4,128)(2,1)}), bf16[32,3,4,1024]{3,2,1,0:T(4,128)(2,1)S(1)}, u32[]{:S(2)}, u32[]{:S(2)}) async-start(bf16[32,3,4,1024]{3,2,1,0:T(4,128)(2,1)} %copy.44), calls=%async_computation | async-start | bytes 1572864 | tf_op jit(solution)/shard_map/all_to_all | solution.py:128
  77.9 15.6 %all-to-all-done = bf16[32,3,4,1024]{3,2,1,0:T(4,128)(2,1)S(1)} async-done(((bf16[32,3,4,1024]{3,2,1,0:T(4,128)(2,1)}), bf16[32,3,4,1024]{3,2,1,0:T(4,128)(2,1)S(1)}, u32[]{:S(2)}, u32[]{:S(2)}) %all-to-all-start) | async-done | bytes 786464 | tf_op jit(solution)/shard_map/all_to_all | solution.py:128
  96.6 2.5 fusion
  99.2 3.7 fusion.2
  102.9 4.0 %fusion.25 = bf16[4,512,64]{1,2,0:T(8,128)(2,1)S(1)} fusion(bf16[4,2048,128]{1,2,0:T(8,128)(2,1)S(1)} %broadcast_select_fusion.1, f32[4,512,2048]{2,1,0:T(8,128)S(1)} %get-tuple-element.49, f32[4,512]{1,0:T(4,128)S(1)} %get-tuple-element.48, pred[2048]{0:T(1024)(128)(4,1)S(1)} %fusion.78, f32[4,512]{1,0:T(4,128)S(1)} %fusion.2), kind=kOutput, calls=%fused_computation.58 | convolution fusion | flops 553910272 | bytes 18106368 | tf_op jit(solution)/shard_map/pqk,pke->pqe/dot_general | solution.py:142
  107.8 16.0 %all_to_all.60 = bf16[1,4,32,1024]{3,1,0,2:T(4,128)(2,1)S(1)} all-to-all(bf16[1,4,32,1024]{3,1,0,2:T(4,128)(2,1)S(1)} %copy.52), channel_id=1, replica_groups=mesh['section'=2,'seq'=32,'cfg'=4] {'seq'}, dimensions={2} | all-to-all | bytes 524288 | tf_op jit(solution)/shard_map/all_to_all | solution.py:150
  124.3 27.8 %all-gather.10.cloned.1.call-done = bf16[1,3072,512]{2,1,0:T(8,128)(2,1)} async-done(((bf16[1,96,512]{2,1,0:T(8,128)(2,1)}), bf16[1,3072,512]{2,1,0:T(8,128)(2,1)}) %all-gather.10.cloned.1.call-update) | async-done | bytes 3145744 | tf_op jit(solution)/shard_map/all_gather | solution.py:89
  152.0 4.6 %copy.54 = bf16[1,3072,512]{1,2,0:T(8,128)(2,1)} copy(bf16[1,3072,512]{2,1,0:T(8,128)(2,1)} %all-gather.10.cloned.1.call-done) | data formatting | bytes 6291456 | tf_op jit(solution)/shard_map/all_gather | solution.py:89
  156.7 4.5 %convolution_bitcast_fusion.1 = f32[4,4,16,3072]{3,2,1,0:T(8,128)} fusion(bf16[4,8,4,16,64]{4,3,2,1,0:T(8,128)(2,1)S(1)} %reshape.453, bf16[3072,8,64,1,1]{0,2,4,1,3:T(8,128)(2,1)} %bitcast.169), kind=kOutput, calls=%fused_computation.15 | convolution fusion | flops 805306368 | bytes 6553600 | tf_op jit(solution)/shard_map/sgpqe,dge->spqd/dot_general | solution.py:153
  161.3 41.5 %reduce-scatter.3.cloned.1.call-done = f32[1,4,16,3072]{3,2,1,0:T(8,128)} async-done(((f32[4,4,16,3072]{3,2,1,0:T(8,128)}), f32[1,4,16,3072]{3,2,1,0:T(8,128)}) %reduce-scatter.3.cloned.1.call-update) | async-done | bytes 786448 | tf_op jit(solution)/shard_map/reduce_scatter | solution.py:152
  207.9 28.5 %all-gather.8.cloned.1.call-done = bf16[4,4,16,3072]{3,2,1,0:T(8,128)(2,1)} async-done(((bf16[1,4,16,3072]{3,2,1,0:T(8,128)(2,1)}), bf16[4,4,16,3072]{3,2,1,0:T(8,128)(2,1)}) %all-gather.8.cloned.1.call-update) | async-done | bytes 1572880 | tf_op jit(solution)/shard_map/all_gather | solution.py:120
  236.4 8.1 %convolution_bitcast_fusion.2 = f32[4,8,3,4,16,64]{5,4,1,3,0,2:T(8,128)S(1)} fusion(bf16[3072,3,8,64,1,1]{0,3,2,5,4,1:T(8,128)(2,1)} %bitcast.168, bf16[4,4,16,3072]{3,2,1,0:T(8,128)(2,1)} %all-gather.8.cloned.1.call-done), kind=kOutput, calls=%fused_computation.18 | convolution fusion | flops 2415919104 | bytes 12582912 | tf_op jit(solution)/shard_map/spqd,djge->sgjpqe/dot_general | solution.py:121
  252.9 30.6 %all_to_all.61 = bf16[32,3,4,1024]{3,2,1,0:T(4,128)(2,1)S(1)} all-to-all(bf16[32,3,4,1024]{3,2,1,0:T(4,128)(2,1)S(1)} %copy.60), channel_id=1, replica_groups=mesh['section'=2,'seq'=32,'cfg'=4] {'seq'}, dimensions={0} | all-to-all | bytes 1572864 | tf_op jit(solution)/shard_map/all_to_all | solution.py:128
  291.1 2.5 fusion.1
  293.6 3.7 fusion.4
  297.3 4.7 %fusion.35 = bf16[4,512,64]{1,2,0:T(8,128)(2,1)} fusion(bf16[4,2048,128]{1,2,0:T(8,128)(2,1)S(1)} %broadcast_select_fusion, f32[4,512,2048]{2,1,0:T(8,128)S(1)} %get-tuple-element.51, f32[4,512]{1,0:T(4,128)S(1)} %get-tuple-element.50, pred[2048]{0:T(1024)(128)(4,1)S(1)} %fusion.78, f32[4,512]{1,0:T(4,128)S(1)} %fusion.4), kind=kOutput, calls=%fused_computation.60 | convolution fusion | flops 553910272 | bytes 18106368 | tf_op jit(solution)/shard_map/pqk,pke->pqe/dot_general | solution.py:142
  303.9 16.0 %all_to_all.62 = bf16[1,4,32,1024]{3,1,0,2:T(4,128)(2,1)S(1)} all-to-all(bf16[1,4,32,1024]{3,1,0,2:T(4,128)(2,1)S(1)} %copy.67), channel_id=1, replica_groups=mesh['section'=2,'seq'=32,'cfg'=4] {'seq'}, dimensions={2} | all-to-all | bytes 524288 | tf_op jit(solution)/shard_map/all_to_all | solution.py:150
  320.2 4.6 %convolution_bitcast_fusion = f32[4,4,16,3072]{3,2,1,0:T(8,128)} fusion(bf16[4,8,4,16,64]{4,3,2,1,0:T(8,128)(2,1)S(1)} %reshape.454, bf16[3072,8,64,1,1]{0,2,4,1,3:T(8,128)(2,1)} %bitcast.170), kind=kOutput, calls=%fused_computation.14 | convolution fusion | flops 805306368 | bytes 6553600 | tf_op jit(solution)/shard_map/sgpqe,dge->spqd/dot_general | solution.py:153
  328.3 34.1 %reduce-scatter.5.cloned.1.call-done = f32[1,4,16,3072]{3,2,1,0:T(8,128)} async-done(((f32[4,4,16,3072]{3,2,1,0:T(8,128)}), f32[1,4,16,3072]{3,2,1,0:T(8,128)}) %reduce-scatter.5.cloned.1.call-update) | async-done | bytes 786448 | tf_op jit(solution)/shard_map/reduce_scatter | solution.py:152
  364.5 22.1 %all-gather.1 = f32[32,16,64]{2,1,0:T(8,128)S(1)} all-gather(f32[4,16,64]{2,1,0:T(8,128)S(1)} %fusion.63), channel_id=3, replica_groups=mesh['section'=2,'seq'=32,'cfg'=4] {'section','cfg'}, dimensions={0}, use_global_device_ids=true | all-gather | bytes 147456 | tf_op jit(solution)/shard_map/all_gather | solution.py:170
  386.6 2.5 fusion.75
  (175 shorter events, 52.0 us)
Async XLA Ops:
  8.0 356.1 %copy-start = (bf16[3072,64]{0,1:T(8,128)(2,1)S(1)}, bf16[3072,64]{0,1:T(8,128)(2,1)}, u32[]{:S(2)}) copy-start(bf16[3072,64]{0,1:T(8,128)(2,1)} %param.19) | copy-start | bytes 1179652
  8.0 39.1 %all-gather.6.cloned.1.call-start = ((), (), s32[]{:S(2)}) async-start(), calls=%async_computation.6 | async-start | bytes 1966080 | tf_op jit(solution)/shard_map/all_gather | solution.py:120
  8.1 18.7 %copy-start.22 = (pred[4,16]{1,0:T(4,128)(4,1)}, pred[4,16]{1,0:T(4,128)(4,1)S(1)}, u32[]{:S(2)}) copy-start(pred[4,16]{1,0:T(4,128)(4,1)S(1)} %add_compare_fusion.1) | copy-start | bytes 196
  62.9 30.6 %all-to-all-start = ((bf16[32,3,4,1024]{3,2,1,0:T(4,128)(2,1)}), bf16[32,3,4,1024]{3,2,1,0:T(4,128)(2,1)S(1)}, u32[]{:S(2)}, u32[]{:S(2)}) async-start(bf16[32,3,4,1024]{3,2,1,0:T(4,128)(2,1)} %copy.44), calls=%async_computation | async-start | bytes 1572864 | tf_op jit(solution)/shard_map/all_to_all | solution.py:128
  72.4 79.6 %all-gather.10.cloned.1.call-start = ((), (), s32[]{:S(2)}) async-start(), calls=%async_computation.10 | async-start | bytes 3244032 | tf_op jit(solution)/shard_map/all_gather | solution.py:89
  73.0 129.8 %reduce-scatter.3.cloned.1.call-start = ((), (), s32[]{:S(2)}) async-start(), calls=%async_computation.7 | async-start | bytes 3932160 | tf_op jit(solution)/shard_map/reduce_scatter | solution.py:152
  124.2 78.7 %copy-start.1 = (bf16[1,4,16,3072]{3,2,1,0:T(8,128)(2,1)S(1)}, bf16[1,4,16,3072]{3,2,1,0:T(8,128)(2,1)}, u32[]{:S(2)}) copy-start(bf16[1,4,16,3072]{3,2,1,0:T(8,128)(2,1)} %param.12) | copy-start | bytes 1179652
  124.2 78.6 %copy-start.10 = (f32[1,1,3072]{2,0,1:T(1,128)S(1)}, f32[1,1,3072]{2,0,1:T(1,128)}, u32[]{:S(2)}) copy-start(f32[1,1,3072]{2,0,1:T(1,128)} %get-tuple-element.35) | copy-start | bytes 36868
  124.2 78.6 %copy-start.23 = (pred[4,16]{1,0:T(4,128)(4,1)S(1)}, pred[4,16]{1,0:T(4,128)(4,1)}, u32[]{:S(2)}) copy-start(pred[4,16]{1,0:T(4,128)(4,1)} %copy-done.22) | copy-start | bytes 196
  124.2 82.4 %copy-start.12 = (f32[1,1,3072]{2,0,1:T(1,128)S(1)}, f32[1,1,3072]{2,0,1:T(1,128)}, u32[]{:S(2)}) copy-start(f32[1,1,3072]{2,0,1:T(1,128)} %copy-done.11) | copy-start | bytes 36868
  124.2 82.4 %copy-start.14 = (f32[1,1,3072]{2,0,1:T(1,128)S(1)}, f32[1,1,3072]{2,0,1:T(1,128)}, u32[]{:S(2)}) copy-start(f32[1,1,3072]{2,0,1:T(1,128)} %copy-done.13) | copy-start | bytes 36868
  124.2 82.4 %copy-start.16 = (f32[1,1,3072]{2,0,1:T(1,128)S(1)}, f32[1,1,3072]{2,0,1:T(1,128)}, u32[]{:S(2)}) copy-start(f32[1,1,3072]{2,0,1:T(1,128)} %copy-done.15) | copy-start | bytes 36868
  124.2 82.4 %copy-start.18 = (f32[1,1,3072]{2,0,1:T(1,128)S(1)}, f32[1,1,3072]{2,0,1:T(1,128)}, u32[]{:S(2)}) copy-start(f32[1,1,3072]{2,0,1:T(1,128)} %copy-done.17) | copy-start | bytes 36868
  161.2 75.2 %all-gather.8.cloned.1.call-start = ((), (), s32[]{:S(2)}) async-start(), calls=%async_computation.8 | async-start | bytes 1966080 | tf_op jit(solution)/shard_map/all_gather | solution.py:120
  204.2 2.1 collective-permute-start
  207.7 154.7 %reduce-scatter.5.cloned.1.call-start = ((), (), s32[]{:S(2)}) async-start(), calls=%async_computation.9 | async-start | bytes 3932160 | tf_op jit(solution)/shard_map/reduce_scatter | solution.py:152
  250.1 36.6 %copy-start.19 = (pred[4,2048]{1,0:T(4,128)(4,1)S(1)}, pred[4,2048]{1,0:T(4,128)(4,1)}, u32[]{:S(2)}) copy-start(pred[4,2048]{1,0:T(4,128)(4,1)} %iota_compare_fusion) | copy-start | bytes 24580
  302.0 22.9 %copy-start.25 = (f32[1,3]{1,0:T(1,128)S(1)}, f32[1,3]{1,0:T(1,128)}, u32[]{:S(2)}) copy-start(f32[1,3]{1,0:T(1,128)} %param.20) | copy-start | bytes 40
  302.0 23.5 %copy-start.21 = (f32[2,3072]{1,0:T(2,128)S(1)}, f32[2,3072]{1,0:T(2,128)}, u32[]{:S(2)}) copy-start(f32[2,3072]{1,0:T(2,128)} %param.18) | copy-start | bytes 73732
  302.0 23.5 %copy-start.3 = (bf16[1,1,4,32,1024]{4,3,2,1,0:T(8,128)(2,1)S(1)}, bf16[1,1,4,32,1024]{4,3,2,1,0:T(8,128)(2,1)}, u32[]{:S(2)}) copy-start(bf16[1,1,4,32,1024]{4,3,2,1,0:T(8,128)(2,1)} %copy-done.2) | copy-start | bytes 786436
  302.0 23.9 %copy-start.5 = (bf16[1,1,4,32,1024]{4,3,2,1,0:T(8,128)(2,1)S(1)}, bf16[1,1,4,32,1024]{4,3,2,1,0:T(8,128)(2,1)}, u32[]{:S(2)}) copy-start(bf16[1,1,4,32,1024]{4,3,2,1,0:T(8,128)(2,1)} %copy-done.4) | copy-start | bytes 786436
  302.0 24.3 %copy-start.7 = (bf16[1,1,4,32,1024]{4,3,2,1,0:T(8,128)(2,1)S(1)}, bf16[1,1,4,32,1024]{4,3,2,1,0:T(8,128)(2,1)}, u32[]{:S(2)}) copy-start(bf16[1,1,4,32,1024]{4,3,2,1,0:T(8,128)(2,1)} %copy-done.6) | copy-start | bytes 786436
  302.0 24.6 %copy-start.9 = (bf16[1,1,4,32,1024]{4,3,2,1,0:T(8,128)(2,1)S(1)}, bf16[1,1,4,32,1024]{4,3,2,1,0:T(8,128)(2,1)}, u32[]{:S(2)}) copy-start(bf16[1,1,4,32,1024]{4,3,2,1,0:T(8,128)(2,1)} %copy-done.8) | copy-start | bytes 786436
  324.8 61.8 %copy-start.20 = (f32[1,4,16,64]{3,2,1,0:T(8,128)S(1)}, f32[1,4,16,64]{3,2,1,0:T(8,128)}, u32[]{:S(2)}) copy-start(f32[1,4,16,64]{3,2,1,0:T(8,128)} %param.13) | copy-start | bytes 49156
  (11 other events, 58.1 us)
Sparse Core Ops, SparseCore 0:
  14.2 32.8 all-gather.5
  161.4 41.4 reduce-scatter.2
  207.8 28.5 all-gather.7
  324.9 37.3 reduce-scatter.4
Sparse Core Ops, SparseCore 1:
  75.5 76.5 all-gather.9
where the time goes:
time: 404 us; the launch traced here: 396 us
  waiting for transfers between devices  169 us (42%)
  blocking collectives  84.7 us (21%)
  local copies, waits for them, and re-layouts  39.7 us (10%)
  matrix products  39.5 us (10%)
  other arithmetic  35.8 us (9%)
  between operations  16.5 us (4%)
  starting transfers between devices  11.1 us (3%)
    reduce_scatter x2, waiting for transfers between devices, run(): lax.psum_scatter(jnp.einsum('sgpqe,dge->spqd', returned, out_full, prefer...  75.6 us
    all_gather x2, waiting for transfers between devices, run(): mixed_rows = lax.all_gather(mixed_rows, 'cfg', axis=0, tiled=True)  48.4 us
    all_to_all x2, blocking collectives, run(): lax.all_to_all(attended, 'seq', split_axis=2, concat_axis=0, tiled=True)  32 us
    all_to_all x1, blocking collectives, run(): lax.all_to_all(outgoing, 'seq', split_axis=0, concat_axis=3, tiled=True)  30.6 us
    all_gather x1, waiting for transfers between devices, per_device(): lax.all_gather(out_weight[0], 'seq', axis=0, tiled=True)  27.8 us
    all_gather x1, blocking collectives, per_device(): lax.all_gather(predicted, ('section', 'cfg'), axis=0, tiled=True)  22.1 us
    dot_general x2, matrix products, run(): jnp.einsum('spqd,djge->sgjpqe', mixed_rows, qkv_full, preferred_element_t...  16.2 us
    all_to_all x1, waiting for transfers between devices, run(): lax.all_to_all(outgoing, 'seq', split_axis=0, concat_axis=3, tiled=True)  15.6 us
  transfers between devices with their start and end apart: 7, of which 7 were waited for; matrix products, arithmetic and copies ran while one was open for 9% of the time, Pallas kernels for 0%

commit v1 on v0

--- a/solution.py
+++ b/solution.py
@@ -6,6 +6,12 @@
 
 HD = 64
 TEXT = 226
+
+
+def tiled_gather(x, axis, dim):
+    size = lax.axis_size(axis)
+    repeats = [size if d == dim else 1 for d in range(x.ndim)]
+    return lax.all_to_all(jnp.tile(x, repeats), axis, split_axis=dim, concat_axis=dim, tiled=True)
 
 
 def from_behind(value, axis, steps):
@@ -86,9 +92,7 @@
     group_heads = qkv_weight.shape[3] // HD
     seq_count = cfg_devices
     qkv_full = qkv_weight[0].reshape(width, 3, group_heads, HD)
-    out_full = lax.all_gather(out_weight[0], "seq", axis=0, tiled=True).reshape(
-        width, group_heads, HD
-    )
+    out_full = tiled_gather(out_weight[0], "seq", 0).reshape(width, group_heads, HD)
     mod_rows = modulation[0]
     stale_rows = stale_cache[0, 0, 0]
     my_sequence = shard_id // group_heads

time: 404 us -> 459 us (1.14)
  waiting for transfers between devices: 169 us -> 210 us
  local copies, waits for them, and re-layouts: 39.7 us -> 53 us
    all_to_all x0 -> x1, waiting for transfers between devices: none -> 66.6 us  [tiled_gather(): lax.all_to_all(jnp.tile(x, repeats), axis, split_axis=dim, concat_axis=di...]
    all_gather x1 -> x0, waiting for transfers between devices: 27.8 us -> none  [per_device(): lax.all_gather(out_weight[0], 'seq', axis=0, tiled=True)]
    reshape x0 -> x1, local copies, waits for them, and re-layouts: none -> 8.59 us  [per_device(): tiled_gather(out_weight[0], 'seq', 0).reshape(width, group_heads, HD)]
    all_to_all x0 -> x1, local copies, waits for them, and re-layouts: none -> 5.72 us  [tiled_gather(): lax.all_to_all(jnp.tile(x, repeats), axis, split_axis=dim, concat_axis=di...]
    all_gather x1 -> x0, local copies, waits for them, and re-layouts: 4.65 us -> none  [per_device(): lax.all_gather(out_weight[0], 'seq', axis=0, tiled=True)]
    unnamed x57 -> x75, local copies, waits for them, and re-layouts: 12.9 us -> 12.9 us
  transfers between devices with their start and end apart: 7 -> 7, of which waited for: 7 -> 7; matrix products, arithmetic and copies ran while one was open for 9% -> 5% of each run, Pallas kernels for 0% -> 0%
where the time goes in v1:
time: 459 us; the launch traced here: 451 us
  waiting for transfers between devices  210 us (46%)
  blocking collectives  84.7 us (18%)
  local copies, waits for them, and re-layouts  53 us (12%)
  matrix products  39 us (8%)
  other arithmetic  34.5 us (8%)
  starting transfers between devices  15.1 us (3%)
  between operations  15.1 us (3%)
    reduce_scatter x2, waiting for transfers between devices, run(): lax.psum_scatter(jnp.einsum('sgpqe,dge->spqd', returned, out_full, prefer...  74.9 us
    all_to_all x1, waiting for transfers between devices, tiled_gather(): lax.all_to_all(jnp.tile(x, repeats), axis, split_axis=dim, concat_axis=di...  66.6 us
    all_gather x2, waiting for transfers between devices, run(): mixed_rows = lax.all_gather(mixed_rows, 'cfg', axis=0, tiled=True)  48.5 us
    all_to_all x2, blocking collectives, run(): lax.all_to_all(attended, 'seq', split_axis=2, concat_axis=0, tiled=True)  32 us
    all_to_all x1, blocking collectives, run(): lax.all_to_all(outgoing, 'seq', split_axis=0, concat_axis=3, tiled=True)  30.6 us
    all_gather x1, blocking collectives, per_device(): lax.all_gather(predicted, ('section', 'cfg'), axis=0, tiled=True)  22.1 us
    all_to_all x1, waiting for transfers between devices, run(): lax.all_to_all(outgoing, 'seq', split_axis=0, concat_axis=3, tiled=True)  18.1 us
    dot_general x2, matrix products, run(): jnp.einsum('spqd,djge->sgjpqe', mixed_rows, qkv_full, preferred_element_t...  16.2 us
  transfers between devices with their start and end apart: 7, of which 7 were waited for; matrix products, arithmetic and copies ran while one was open for 5% of the time, Pallas kernels for 0%

profile of v1, /device:TPU:1, one launch (start us, length us, event | category | flops | bytes accessed | tf_op | source)
XLA Modules:
  0.0 451.0 jit_solution(5998155164784358680)
XLA Ops:
  13.3 12.7 %copy.39 = bf16[1,3072,3,512]{1,3,2,0:T(8,128)(2,1)} copy(bf16[1,3072,3,512]{3,1,2,0:T(8,128)(2,1)} %param.15) | data formatting | bytes 18874368 | tf_op args[3]
  26.4 19.9 %all-gather.4.cloned.1.call-done = bf16[4,4,16,3072]{3,2,1,0:T(8,128)(2,1)} async-done(((bf16[1,4,16,3072]{3,2,1,0:T(8,128)(2,1)}), bf16[4,4,16,3072]{3,2,1,0:T(8,128)(2,1)}) %all-gather.4.cloned.1.call-update) | async-done | bytes 1572880 | tf_op jit(solution)/shard_map/all_gather | solution.py:124
  46.3 8.1 %convolution_bitcast_fusion.3 = f32[4,8,3,4,16,64]{5,4,1,2,3,0:T(8,128)S(1)} fusion(bf16[3072,3,8,64,1,1]{0,3,2,1,5,4:T(8,128)(2,1)} %bitcast.168, bf16[4,4,16,3072]{3,2,1,0:T(8,128)(2,1)} %all-gather.4.cloned.1.call-done), kind=kOutput, calls=%fused_computation.21 | convolution fusion | flops 2415919104 | bytes 12582912 | tf_op jit(solution)/shard_map/spqd,djge->sgjpqe/dot_general | solution.py:125
  62.2 10.0 %all-to-all-start = ((bf16[32,3,4,1024]{3,2,1,0:T(4,128)(2,1)}), bf16[32,3,4,1024]{3,2,1,0:T(4,128)(2,1)S(1)}, u32[]{:S(2)}, u32[]{:S(2)}) async-start(bf16[32,3,4,1024]{3,2,1,0:T(4,128)(2,1)} %copy.44), calls=%async_computation | async-start | bytes 1572864 | tf_op jit(solution)/shard_map/all_to_all | solution.py:132
  75.1 18.1 %all-to-all-done = bf16[32,3,4,1024]{3,2,1,0:T(4,128)(2,1)S(1)} async-done(((bf16[32,3,4,1024]{3,2,1,0:T(4,128)(2,1)}), bf16[32,3,4,1024]{3,2,1,0:T(4,128)(2,1)S(1)}, u32[]{:S(2)}, u32[]{:S(2)}) %all-to-all-start) | async-done | bytes 786464 | tf_op jit(solution)/shard_map/all_to_all | solution.py:132
  98.2 3.7 fusion.2
  101.9 4.0 fusion.27
  106.8 16.1 %all_to_all.66 = bf16[1,4,32,1024]{3,1,0,2:T(4,128)(2,1)} all-to-all(bf16[1,4,32,1024]{3,1,0,2:T(4,128)(2,1)S(1)} %copy.52), channel_id=1, replica_groups=mesh['section'=2,'seq'=32,'cfg'=4] {'seq'}, dimensions={2} | all-to-all | bytes 524288 | tf_op jit(solution)/shard_map/all_to_all | solution.py:154
  124.9 4.1 all-to-all-start.2
  131.1 66.6 %all-to-all-done.2 = bf16[32,96,512]{2,1,0:T(8,128)(2,1)S(1)} async-done(((bf16[32,96,512]{2,1,0:T(8,128)(2,1)}), bf16[32,96,512]{2,1,0:T(8,128)(2,1)S(1)}, u32[]{:S(2)}, u32[]{:S(2)}) %all-to-all-start.2) | async-done | bytes 3145760 | tf_op jit(solution)/shard_map/all_to_all | solution.py:14
  197.7 5.7 %copy.54 = bf16[32,96,512]{1,0,2:T(8,128)(2,1)} copy(bf16[32,96,512]{2,1,0:T(8,128)(2,1)S(1)} %all-to-all-done.2) | data formatting | bytes 6291456 | tf_op jit(solution)/shard_map/all_to_all | solution.py:14
  203.4 8.6 %reshape.454 = bf16[3072,8,64,1,1]{0,2,1,3,4:T(8,128)(2,1)} reshape(bf16[32,96,512]{1,0,2:T(8,128)(2,1)} %copy.54) | data formatting | bytes 6291456 | tf_op jit(solution)/shard_map/reshape | solution.py:95
  212.0 4.8 %convolution_bitcast_fusion.1 = f32[4,4,16,3072]{3,2,1,0:T(8,128)} fusion(bf16[4,8,4,16,64]{4,3,2,1,0:T(8,128)(2,1)} %reshape.459, bf16[3072,8,64,1,1]{0,2,1,3,4:T(8,128)(2,1)} %reshape.454), kind=kOutput, calls=%fused_computation.15 | convolution fusion | flops 805306368 | bytes 6553600 | tf_op jit(solution)/shard_map/sgpqe,dge->spqd/dot_general | solution.py:157
  217.1 40.8 %reduce-scatter.3.cloned.1.call-done = f32[1,4,16,3072]{3,2,1,0:T(8,128)} async-done(((f32[4,4,16,3072]{3,2,1,0:T(8,128)}), f32[1,4,16,3072]{3,2,1,0:T(8,128)}) %reduce-scatter.3.cloned.1.call-update) | async-done | bytes 786448 | tf_op jit(solution)/shard_map/reduce_scatter | solution.py:156
  262.8 28.7 %all-gather.6.cloned.1.call-done = bf16[4,4,16,3072]{3,2,1,0:T(8,128)(2,1)} async-done(((bf16[1,4,16,3072]{3,2,1,0:T(8,128)(2,1)}), bf16[4,4,16,3072]{3,2,1,0:T(8,128)(2,1)}) %all-gather.6.cloned.1.call-update) | async-done | bytes 1572880 | tf_op jit(solution)/shard_map/all_gather | solution.py:124
  291.4 8.1 %convolution_bitcast_fusion.2 = f32[4,8,3,4,16,64]{5,4,1,3,0,2:T(8,128)S(1)} fusion(bf16[3072,3,8,64,1,1]{0,3,2,5,4,1:T(8,128)(2,1)} %bitcast.169, bf16[4,4,16,3072]{3,2,1,0:T(8,128)(2,1)} %all-gather.6.cloned.1.call-done), kind=kOutput, calls=%fused_computation.20 | convolution fusion | flops 2415919104 | bytes 12582912 | tf_op jit(solution)/shard_map/spqd,djge->sgjpqe/dot_general | solution.py:125
  309.8 30.6 %all_to_all.67 = bf16[32,3,4,1024]{3,2,1,0:T(4,128)(2,1)S(1)} all-to-all(bf16[32,3,4,1024]{3,2,1,0:T(4,128)(2,1)S(1)} %copy.60), channel_id=1, replica_groups=mesh['section'=2,'seq'=32,'cfg'=4] {'seq'}, dimensions={0} | all-to-all | bytes 1572864 | tf_op jit(solution)/shard_map/all_to_all | solution.py:132
  348.0 2.5 fusion.1
  350.5 3.7 fusion.4
  354.2 4.0 fusion.37
  359.2 16.0 %all_to_all.68 = bf16[1,4,32,1024]{3,1,0,2:T(4,128)(2,1)S(1)} all-to-all(bf16[1,4,32,1024]{3,1,0,2:T(4,128)(2,1)S(1)} %copy.67), channel_id=1, replica_groups=mesh['section'=2,'seq'=32,'cfg'=4] {'seq'}, dimensions={2} | all-to-all | bytes 524288 | tf_op jit(solution)/shard_map/all_to_all | solution.py:154
  375.5 4.6 %convolution_bitcast_fusion = f32[4,4,16,3072]{3,2,1,0:T(8,128)} fusion(bf16[4,8,4,16,64]{4,3,2,1,0:T(8,128)(2,1)S(1)} %reshape.461, bf16[3072,8,64,1,1]{0,2,1,3,4:T(8,128)(2,1)} %reshape.454), kind=kOutput, calls=%fused_computation.14 | convolution fusion | flops 805306368 | bytes 6553600 | tf_op jit(solution)/shard_map/sgpqe,dge->spqd/dot_general | solution.py:157
  383.5 34.1 %reduce-scatter.5.cloned.1.call-done = f32[1,4,16,3072]{3,2,1,0:T(8,128)} async-done(((f32[4,4,16,3072]{3,2,1,0:T(8,128)}), f32[1,4,16,3072]{3,2,1,0:T(8,128)}) %reduce-scatter.5.cloned.1.call-update) | async-done | bytes 786448 | tf_op jit(solution)/shard_map/reduce_scatter | solution.py:156
  419.7 22.1 %all-gather = f32[32,16,64]{2,1,0:T(8,128)S(1)} all-gather(f32[4,16,64]{2,1,0:T(8,128)S(1)} %fusion.65), channel_id=2, replica_groups=mesh['section'=2,'seq'=32,'cfg'=4] {'section','cfg'}, dimensions={0}, use_global_device_ids=true | all-gather | bytes 147456 | tf_op jit(solution)/shard_map/all_gather | solution.py:174
  (194 shorter events, 58.3 us)
Async XLA Ops:
  7.2 412.2 %copy-start = (bf16[3072,64]{0,1:T(8,128)(2,1)S(1)}, bf16[3072,64]{0,1:T(8,128)(2,1)}, u32[]{:S(2)}) copy-start(bf16[3072,64]{0,1:T(8,128)(2,1)} %param.19) | copy-start | bytes 1179652
  7.2 39.1 %all-gather.4.cloned.1.call-start = ((), (), s32[]{:S(2)}) async-start(), calls=%async_computation.7 | async-start | bytes 1966080 | tf_op jit(solution)/shard_map/all_gather | solution.py:124
  62.2 31.1 %all-to-all-start = ((bf16[32,3,4,1024]{3,2,1,0:T(4,128)(2,1)}), bf16[32,3,4,1024]{3,2,1,0:T(4,128)(2,1)S(1)}, u32[]{:S(2)}, u32[]{:S(2)}) async-start(bf16[32,3,4,1024]{3,2,1,0:T(4,128)(2,1)} %copy.44), calls=%async_computation | async-start | bytes 1572864 | tf_op jit(solution)/shard_map/all_to_all | solution.py:132
  72.4 25.8 %copy-start.2 = (bf16[2048,128]{0,1:T(8,128)(2,1)}, bf16[2048,128]{0,1:T(8,128)(2,1)S(1)}, u32[]{:S(2)}) copy-start(bf16[2048,128]{0,1:T(8,128)(2,1)S(1)} %copy.49) | copy-start | bytes 1572868
  75.1 23.1 %copy-start.27 = (pred[4,2048]{1,0:T(4,128)(4,1)}, pred[4,2048]{1,0:T(4,128)(4,1)S(1)}, u32[]{:S(2)}) copy-start(pred[4,2048]{1,0:T(4,128)(4,1)S(1)} %iota_compare_fusion) | copy-start | bytes 24580
  124.9 72.8 %all-to-all-start.2 = ((bf16[32,96,512]{2,1,0:T(8,128)(2,1)}), bf16[32,96,512]{2,1,0:T(8,128)(2,1)S(1)}, u32[]{:S(2)}, u32[]{:S(2)}) async-start(bf16[32,96,512]{2,1,0:T(8,128)(2,1)} %tile.9), calls=%async_computation.2 | async-start | bytes 6291456 | tf_op jit(solution)/shard_map/all_to_all | solution.py:14
  129.0 128.9 %reduce-scatter.3.cloned.1.call-start = ((), (), s32[]{:S(2)}) async-start(), calls=%async_computation.8 | async-start | bytes 3932160 | tf_op jit(solution)/shard_map/reduce_scatter | solution.py:156
  203.4 54.4 %copy-start.1 = (bf16[1,4,16,3072]{3,2,1,0:T(8,128)(2,1)S(1)}, bf16[1,4,16,3072]{3,2,1,0:T(8,128)(2,1)}, u32[]{:S(2)}) copy-start(bf16[1,4,16,3072]{3,2,1,0:T(8,128)(2,1)} %param.12) | copy-start | bytes 1179652
  203.4 54.4 %copy-start.17 = (f32[1,1,3072]{2,0,1:T(1,128)S(1)}, f32[1,1,3072]{2,0,1:T(1,128)}, u32[]{:S(2)}) copy-start(f32[1,1,3072]{2,0,1:T(1,128)} %get-tuple-element.35) | copy-start | bytes 36868
  203.4 54.4 %copy-start.32 = (pred[4,16]{1,0:T(4,128)(4,1)S(1)}, pred[4,16]{1,0:T(4,128)(4,1)}, u32[]{:S(2)}) copy-start(pred[4,16]{1,0:T(4,128)(4,1)} %copy-done.31) | copy-start | bytes 196
  212.0 49.6 %copy-start.19 = (f32[1,1,3072]{2,0,1:T(1,128)S(1)}, f32[1,1,3072]{2,0,1:T(1,128)}, u32[]{:S(2)}) copy-start(f32[1,1,3072]{2,0,1:T(1,128)} %copy-done.18) | copy-start | bytes 36868
  212.0 49.6 %copy-start.21 = (f32[1,1,3072]{2,0,1:T(1,128)S(1)}, f32[1,1,3072]{2,0,1:T(1,128)}, u32[]{:S(2)}) copy-start(f32[1,1,3072]{2,0,1:T(1,128)} %copy-done.20) | copy-start | bytes 36868
  212.0 49.6 %copy-start.23 = (f32[1,1,3072]{2,0,1:T(1,128)S(1)}, f32[1,1,3072]{2,0,1:T(1,128)}, u32[]{:S(2)}) copy-start(f32[1,1,3072]{2,0,1:T(1,128)} %copy-done.22) | copy-start | bytes 36868
  212.0 49.6 %copy-start.25 = (f32[1,1,3072]{2,0,1:T(1,128)S(1)}, f32[1,1,3072]{2,0,1:T(1,128)}, u32[]{:S(2)}) copy-start(f32[1,1,3072]{2,0,1:T(1,128)} %copy-done.24) | copy-start | bytes 36868
  216.8 74.6 %all-gather.6.cloned.1.call-start = ((), (), s32[]{:S(2)}) async-start(), calls=%async_computation.9 | async-start | bytes 1966080 | tf_op jit(solution)/shard_map/all_gather | solution.py:124
  259.2 2.1 collective-permute-start
  262.7 154.9 %reduce-scatter.5.cloned.1.call-start = ((), (), s32[]{:S(2)}) async-start(), calls=%async_computation.10 | async-start | bytes 3932160 | tf_op jit(solution)/shard_map/reduce_scatter | solution.py:156
  306.0 37.6 %copy-start.3 = (bf16[2048,128]{0,1:T(8,128)(2,1)S(1)}, bf16[2048,128]{0,1:T(8,128)(2,1)}, u32[]{:S(2)}) copy-start(bf16[2048,128]{0,1:T(8,128)(2,1)} %copy-done.2) | copy-start | bytes 1572868
  306.0 37.6 %copy-start.28 = (pred[4,2048]{1,0:T(4,128)(4,1)S(1)}, pred[4,2048]{1,0:T(4,128)(4,1)}, u32[]{:S(2)}) copy-start(pred[4,2048]{1,0:T(4,128)(4,1)} %copy-done.27) | copy-start | bytes 24580
  358.3 22.4 %copy-start.5 = (bf16[1,1,4,32,1024]{4,3,2,1,0:T(8,128)(2,1)S(1)}, bf16[1,1,4,32,1024]{4,3,2,1,0:T(8,128)(2,1)}, u32[]{:S(2)}) copy-start(bf16[1,1,4,32,1024]{4,3,2,1,0:T(8,128)(2,1)} %copy-done.4) | copy-start | bytes 786436
  358.3 22.8 %copy-start.7 = (bf16[1,1,4,32,1024]{4,3,2,1,0:T(8,128)(2,1)S(1)}, bf16[1,1,4,32,1024]{4,3,2,1,0:T(8,128)(2,1)}, u32[]{:S(2)}) copy-start(bf16[1,1,4,32,1024]{4,3,2,1,0:T(8,128)(2,1)} %copy-done.6) | copy-start | bytes 786436
  358.3 23.1 %copy-start.9 = (bf16[1,1,4,32,1024]{4,3,2,1,0:T(8,128)(2,1)S(1)}, bf16[1,1,4,32,1024]{4,3,2,1,0:T(8,128)(2,1)}, u32[]{:S(2)}) copy-start(bf16[1,1,4,32,1024]{4,3,2,1,0:T(8,128)(2,1)} %copy-done.8) | copy-start | bytes 786436
  358.3 23.5 %copy-start.11 = (bf16[1,1,4,32,1024]{4,3,2,1,0:T(8,128)(2,1)S(1)}, bf16[1,1,4,32,1024]{4,3,2,1,0:T(8,128)(2,1)}, u32[]{:S(2)}) copy-start(bf16[1,1,4,32,1024]{4,3,2,1,0:T(8,128)(2,1)} %copy-done.10) | copy-start | bytes 786436
  380.1 61.7 %copy-start.29 = (f32[1,4,16,64]{3,2,1,0:T(8,128)S(1)}, f32[1,4,16,64]{3,2,1,0:T(8,128)}, u32[]{:S(2)}) copy-start(f32[1,4,16,64]{3,2,1,0:T(8,128)} %param.13) | copy-start | bytes 49156
  (20 other events, 163.8 us)
Sparse Core Ops, SparseCore 0:
  13.4 32.8 all-gather.3
  217.0 40.8 reduce-scatter.2
  262.9 28.5 all-gather.5
  380.2 37.3 reduce-scatter.4
